TPU v7x, 128 devices: a whole 4x4x4 slice. The times are simulated.
128 devices in a mesh: row: 16 (over z, y), col: 8 (over x, core).
Axes of the slice: x: 4, y: 4, z: 4, core: 2. Of those that a mesh axis runs over, the one named last changes fastest.
Arguments:
- queries: float32 [32768, 256], P(('row', 'col')), may hold values from -1 to 1
- passages: float32 [32768, 256], P(('col', 'row')), may hold values from -1 to 1
- mean_cost: float32 [1], replicated, may hold values from 1 to 3
Outputs:
- row_potential: float32 [32768], P('row')
- col_potential: float32 [32768], P('col')
All inputs are finite; a program needn't handle non-finite values.
Results may differ from a plain program's by a relative error of at most 0.0003.
Values sent between devices are 32-bit elements; how exact they have to be, the bound alone decides.
No kernel may reach another device: no remote copies, remote signals or barrier semaphores. Data moves between devices by JAX's collectives and lax.ppermute only.
A program may use at most 256 MiB of HBM per device.

v0:
```python
import math
import jax
import jax.numpy as jnp
from jax import lax
from jax.sharding import PartitionSpec as P

ITERS = 3


def inner_costs(left, right):
    left_norms = jnp.sum(left * left, axis=1)
    right_norms = jnp.sum(right * right, axis=1)
    inner = lax.dot_general(
        left,
        right,
        (((1,), (1,)), ((), ())),
        precision=lax.Precision.HIGHEST,
        preferred_element_type=jnp.float32,
    )
    return left_norms[:, None] + right_norms[None, :] - 2.0 * inner


def digit_partners(axis, size, stride, width, shift):
    perm = []
    for i in range(size):
        p = i // stride % width
        perm.append((i, i + ((p + shift) % width - p) * stride))
    return perm


def exchange(x, axis, stride, width):
    size = lax.axis_size(axis)
    pos = lax.axis_index(axis) // stride % width
    received = [x] + [
        lax.ppermute(x, axis, digit_partners(axis, size, stride, width, k)) for k in range(1, width)
    ]
    stacked = jnp.stack(received)
    return [
        lax.dynamic_index_in_dim(stacked, (pos - q) % width, 0, keepdims=False)
        for q in range(width)
    ]


def combine_over(peak, total, axis, digits):
    size = lax.axis_size(axis)
    packed = jnp.stack([peak, total])
    stride = 1
    for width in digits:
        parts = [packed] + [
            lax.ppermute(packed, axis, digit_partners(axis, size, stride, width, k))
            for k in range(1, width)
        ]
        new_peak = parts[0][0]
        for part in parts[1:]:
            new_peak = jnp.maximum(new_peak, part[0])
        terms = [part[1] * jnp.exp(part[0] - new_peak) for part in parts]
        if width == 4:
            new_total = terms[0] + terms[2] + (terms[1] + terms[3])
        else:
            new_total = terms[0] + terms[1]
        packed = jnp.stack([new_peak, new_total])
        stride *= width
    return packed[0] + jnp.log(packed[1])


def radix_digits(size):
    digits = []
    while size > 1:
        width = 4 if size % 4 == 0 else 2
        digits.append(width)
        size //= width
    return tuple(digits)


def col_digits(size):
    if size % 2 == 0:
        return (2,) + radix_digits(size // 2)
    return radix_digits(size)


def logsum_col(gaps, scale):
    peak = jnp.max(gaps, axis=1) / scale
    totals = jnp.sum(jnp.exp(gaps / scale - peak[:, None]), axis=1)
    return combine_over(peak, totals, "col", col_digits(lax.axis_size("col")))


def logsum_row(gaps, scale):
    peak = jnp.max(gaps, axis=0) / scale
    totals = jnp.sum(jnp.exp(gaps / scale - peak[None, :]), axis=0)
    return combine_over(peak, totals, "row", radix_digits(lax.axis_size("row")))


def gather_col(x):
    size = lax.axis_size("col")
    return jnp.concatenate(exchange(x, "col", 1, size), axis=0)


def gather_row(x):
    stride = 1
    for width in radix_digits(lax.axis_size("row")):
        x = jnp.concatenate(exchange(x, "row", stride, width), axis=0)
        stride *= width
    return x


def per_device(queries, passages, mean_cost):
    entropy_scale = 0.1 * mean_cost[0]
    row_count = lax.axis_size("row")
    col_count = lax.axis_size("col")
    all_queries = queries.shape[0] * row_count * col_count
    all_passages = passages.shape[0] * row_count * col_count
    query_block = gather_col(queries)
    rows = passages.shape[0]
    split = rows - rows * 5 // 32
    passage_block = jnp.concatenate(
        [lax.all_gather(passages[:split], "row", axis=0, tiled=True), gather_row(passages[split:])],
        axis=0,
    )
    cost_tile = inner_costs(query_block, passage_block)
    col_potential = jnp.zeros((cost_tile.shape[1],), jnp.float32)
    row_potential = jnp.zeros((cost_tile.shape[0],), jnp.float32)
    for repeat in range(ITERS):
        gaps = col_potential[None, :] - cost_tile
        row_potential = -entropy_scale * math.log(all_queries) - entropy_scale * logsum_col(
            gaps, entropy_scale
        )
        gaps = row_potential[:, None] - cost_tile
        col_potential = -entropy_scale * math.log(all_passages) - entropy_scale * logsum_row(
            gaps, entropy_scale
        )
    head = col_potential[: split * row_count].reshape(row_count, split)
    tail = col_potential[split * row_count :].reshape(row_count, rows - split)
    return (row_potential, jnp.concatenate([head, tail], axis=1).reshape(-1))


def solution(mesh):
    placed = (P(("row", "col"), None), P(("col", "row"), None), P())
    return jax.shard_map(
        per_device, mesh=mesh, in_specs=placed, out_specs=(P("row"), P("col")), check_vma=False
    )
```

profile of v0, /device:TPU:0, one launch (start us, length us, event | category | flops | bytes accessed | tf_op | source)
XLA Modules:
  0.0 269.4 jit_solution(6732371264932919641)
XLA Ops:
  7.2 1.7 slice.222
  9.7 1.7 collective-permute-start.7
  11.4 2.9 %collective-permute-start.8 = (f32[40,256]{1,0:T(8,128)S(1)}, f32[40,256]{1,0:T(8,128)S(1)}, u32[]{:S(2)}, u32[]{:S(2)}) collective-permute-start(f32[40,256]{1,0:T(8,128)S(1)} %get-tuple-element.7), channel_id=1, source_target_pairs={{0,16},{8,24},{16,0},{24,8},{32,48},{40,56},{48,32},{56,40},{64,80... | collective-permute-start | bytes 122888 | tf_op jit(solution)/shard_map/ppermute | solution.py:35
  14.3 1.3 collective-permute-start.9
  15.6 1.5 collective-permute-start.1
  18.4 2.0 collective-permute-start.10
  20.4 3.6 %collective-permute-start.11 = (f32[160,256]{1,0:T(8,128)S(1)}, f32[160,256]{1,0:T(8,128)S(1)}, u32[]{:S(2)}, u32[]{:S(2)}) collective-permute-start(f32[160,256]{1,0:T(8,128)S(1)} %get-tuple-element.9), channel_id=1, source_target_pairs={{0,64},{8,72},{16,80},{24,88},{32,96},{40,104},{48,112},{56,120},{... | collective-permute-start | bytes 491528 | tf_op jit(solution)/shard_map/ppermute | solution.py:35
  25.9 1.9 collective-permute-done.10
  27.8 1.5 collective-permute-start.2
  29.3 5.5 %collective-permute-done.11 = f32[160,256]{1,0:T(8,128)S(1)} collective-permute-done((f32[160,256]{1,0:T(8,128)S(1)}, f32[160,256]{1,0:T(8,128)S(1)}, u32[]{:S(2)}, u32[]{:S(2)}) %collective-permute-start.11) | collective-permute-done | bytes 163872 | tf_op jit(solution)/shard_map/ppermute | solution.py:35
  34.8 1.3 collective-permute-start.3
  36.1 1.6 collective-permute-start.4
  37.8 1.2 collective-permute-start.5
  39.8 5.0 %collective-permute-done.3 = f32[256,256]{1,0:T(8,128)S(1)} collective-permute-done((f32[256,256]{1,0:T(8,128)}, f32[256,256]{1,0:T(8,128)S(1)}, u32[]{:S(2)}, u32[]{:S(2)}) %collective-permute-start.3) | collective-permute-done | bytes 262176 | tf_op jit(solution)/shard_map/ppermute | solution.py:35
  45.6 7.9 %collective-permute-done.5 = f32[256,256]{1,0:T(8,128)S(1)} collective-permute-done((f32[256,256]{1,0:T(8,128)S(1)}, f32[256,256]{1,0:T(8,128)S(1)}, u32[]{:S(2)}, u32[]{:S(2)}) %collective-permute-start.5) | collective-permute-done | bytes 262176 | tf_op jit(solution)/shard_map/ppermute | solution.py:35
  53.6 2.0 collective-permute-done.6
  56.2 7.0 %all-gather.2.cloned.1.call-done = f32[3456,256]{1,0:T(8,128)} async-done(((f32[216,256]{1,0:T(8,128)}), f32[3456,256]{1,0:T(8,128)}) %all-gather.2.cloned.1.call-update) | async-done | bytes 3538960 | tf_op jit(solution)/shard_map/all_gather | solution.py:116
  63.2 2.2 constant_dynamic-update-slice_fusion
  66.2 34.8 %subtract_reduce_fusion.5 = (f32[2048]{0:T(1024)S(1)}, f32[2048,4096]{1,0:T(8,128)}) fusion(f32[2048,256]{1,0:T(8,128)S(1)} %bitcast_dynamic-update-slice_fusion, f32[4096,256]{1,0:T(8,128)S(1)} %bitcast_dynamic-update-slice_fusion.16, f32[4096]{0:T(1024)S(1)} %multiply_reduce_fusion, f32[2048]{0:T(1024)S(1)} %multiply_reduce_fusion.1), kind=kOutput, calls=%fused_computation.12 | convolution fusion | flops 25811744768 | bytes 39878656 | tf_op jit(solution)/shard_map/dot_general | solution.py:13
  101.0 14.5 %exponential_reduce_fusion.5 = f32[2048]{0:T(1024)S(1)} fusion(f32[2048,4096]{1,0:T(8,128)} %get-tuple-element.59, f32[2048]{0:T(1024)S(1)} %broadcast_divide_fusion.5, f32[]{:T(128)} %bitcast), kind=kLoop, calls=%fused_computation.5 | loop fusion | flops 33552384 | bytes 33570820 | tf_op jit(solution)/shard_map/reduce_sum | solution.py:83
  115.6 1.2 collective-permute-done.13
  116.9 1.5 collective-permute-start.14
  118.4 2.7 collective-permute-start.15
  121.1 1.5 collective-permute-start.16
  122.6 1.1 collective-permute-done.15
  123.7 1.2 collective-permute-done.16
  124.9 13.8 %subtract_reduce_fusion.4 = f32[4096]{0:T(1024)S(1)} fusion(f32[2048,4096]{1,0:T(8,128)} %get-tuple-element.59, f32[2048]{0:T(1024)S(1)} %multiply_subtract_fusion.6), kind=kLoop, calls=%fused_computation.11 | loop fusion | flops 16773120 | bytes 33579008 | tf_op jit(solution)/shard_map/reduce_max | solution.py:88
  138.7 6.3 %copy-done = f32[2048,4096]{1,0:T(8,128)S(1)} copy-done((f32[2048,4096]{1,0:T(8,128)S(1)}, f32[2048,4096]{1,0:T(8,128)}, u32[]{:S(2)}) %copy-start) | copy-done | bytes 33554456
  145.0 7.6 %exponential_reduce_fusion.4 = f32[4096]{0:T(1024)S(1)} fusion(f32[2048,4096]{1,0:T(8,128)S(1)} %copy-done, f32[4096]{0:T(1024)S(1)} %broadcast_divide_fusion.2, f32[2048]{0:T(1024)S(1)} %multiply_subtract_fusion.6, f32[]{:T(128)} %bitcast), kind=kLoop, calls=%fused_computation.4 | loop fusion | flops 33550336 | bytes 33595396 | tf_op jit(solution)/shard_map/reduce_sum | solution.py:89
  153.5 2.7 %collective-permute-start.18 = (f32[2,4096]{1,0:T(2,128)S(1)}, f32[2,4096]{1,0:T(2,128)S(1)}, u32[]{:S(2)}, u32[]{:S(2)}) collective-permute-start(f32[2,4096]{1,0:T(2,128)S(1)} %pad_maximum_fusion.3), channel_id=1, source_target_pairs={{0,16},{8,24},{16,0},{24,8},{32,48},{40,56},{48,32},{56,40},{64,80... | collective-permute-start | bytes 98312 | tf_op jit(solution)/shard_map/ppermute | solution.py:50
  156.2 1.4 collective-permute-start.19
  158.9 1.2 collective-permute-done.19
  160.5 2.6 collective-permute-start.21
  163.1 1.4 collective-permute-start.22
  166.0 1.1 collective-permute-done.22
  167.2 3.0 %subtract_reduce_fusion.3 = f32[2048]{0:T(1024)S(1)} fusion(f32[2048,4096]{1,0:T(8,128)S(1)} %copy-done, f32[4096]{0:T(1024)S(1)} %bitcast.126), kind=kLoop, calls=%fused_computation.10 | loop fusion | flops 16775168 | bytes 33579008 | tf_op jit(solution)/shard_map/reduce_max | solution.py:82
  170.2 8.0 %exponential_reduce_fusion.3 = f32[2048]{0:T(1024)S(1)} fusion(f32[2048,4096]{1,0:T(8,128)S(1)} %copy-done, f32[2048]{0:T(1024)S(1)} %broadcast_divide_fusion.4, f32[4096]{0:T(1024)S(1)} %bitcast.127, f32[]{:T(128)} %bitcast), kind=kLoop, calls=%fused_computation.3 | loop fusion | flops 33552384 | bytes 33587204 | tf_op jit(solution)/shard_map/reduce_sum | solution.py:83
  178.3 1.2 collective-permute-done.23
  180.0 3.8 %collective-permute-start.25 = (f32[2,2048]{1,0:T(2,128)S(1)}, f32[2,2048]{1,0:T(2,128)S(1)}, u32[]{:S(2)}, u32[]{:S(2)}) collective-permute-start(f32[2,2048]{1,0:T(2,128)S(1)} %pad_maximum_fusion.12), channel_id=1, source_target_pairs={{0,4},{1,5},{2,6},{3,7},{4,0},{5,1},{6,2},{7,3},{8,12},{9,13},{10,... | collective-permute-start | bytes 49160 | tf_op jit(solution)/shard_map/ppermute | solution.py:50
  185.7 1.8 collective-permute-done.26
  187.6 4.7 %subtract_reduce_fusion.2 = f32[4096]{0:T(1024)S(1)} fusion(f32[2048,4096]{1,0:T(8,128)S(1)} %copy-done, f32[2048]{0:T(1024)S(1)} %multiply_subtract_fusion.5), kind=kLoop, calls=%fused_computation.9 | loop fusion | flops 16773120 | bytes 33579008 | tf_op jit(solution)/shard_map/reduce_max | solution.py:88
  192.3 7.6 %exponential_reduce_fusion.2 = f32[4096]{0:T(1024)S(1)} fusion(f32[2048,4096]{1,0:T(8,128)S(1)} %copy-done, f32[4096]{0:T(1024)S(1)} %broadcast_divide_fusion.1, f32[2048]{0:T(1024)S(1)} %multiply_subtract_fusion.5, f32[]{:T(128)} %bitcast), kind=kLoop, calls=%fused_computation.2 | loop fusion | flops 33550336 | bytes 33595396 | tf_op jit(solution)/shard_map/reduce_sum | solution.py:89
  200.0 1.4 collective-permute-start.27
  201.5 2.7 %collective-permute-start.28 = (f32[2,4096]{1,0:T(2,128)S(1)}, f32[2,4096]{1,0:T(2,128)S(1)}, u32[]{:S(2)}, u32[]{:S(2)}) collective-permute-start(f32[2,4096]{1,0:T(2,128)S(1)} %pad_maximum_fusion.5), channel_id=1, source_target_pairs={{0,16},{8,24},{16,0},{24,8},{32,48},{40,56},{48,32},{56,40},{64,80... | collective-permute-start | bytes 98312 | tf_op jit(solution)/shard_map/ppermute | solution.py:50
  205.2 1.7 collective-permute-done.28
  206.9 1.2 collective-permute-done.29
  208.3 1.4 collective-permute-start.30
  209.7 2.7 collective-permute-start.31
  213.5 1.7 collective-permute-done.31
  215.1 1.2 collective-permute-done.32
  216.5 3.0 %subtract_reduce_fusion.1 = f32[2048]{0:T(1024)S(1)} fusion(f32[2048,4096]{1,0:T(8,128)S(1)} %copy-done, f32[4096]{0:T(1024)S(1)} %bitcast.128), kind=kLoop, calls=%fused_computation.8 | loop fusion | flops 16775168 | bytes 33579008 | tf_op jit(solution)/shard_map/reduce_max | solution.py:82
  219.5 8.0 %exponential_reduce_fusion.1 = f32[2048]{0:T(1024)S(1)} fusion(f32[2048,4096]{1,0:T(8,128)S(1)} %copy-done, f32[2048]{0:T(1024)S(1)} %broadcast_divide_fusion.3, f32[4096]{0:T(1024)S(1)} %bitcast.129, f32[]{:T(128)} %bitcast), kind=kLoop, calls=%fused_computation.1 | loop fusion | flops 33552384 | bytes 33587204 | tf_op jit(solution)/shard_map/reduce_sum | solution.py:83
  227.6 1.2 collective-permute-done.33
  229.0 2.7 %collective-permute-start.35 = (f32[2,2048]{1,0:T(2,128)S(1)}, f32[2,2048]{1,0:T(2,128)S(1)}, u32[]{:S(2)}, u32[]{:S(2)}) collective-permute-start(f32[2,2048]{1,0:T(2,128)S(1)} %pad_maximum_fusion.14), channel_id=1, source_target_pairs={{0,4},{1,5},{2,6},{3,7},{4,0},{5,1},{6,2},{7,3},{8,12},{9,13},{10,... | collective-permute-start | bytes 49160 | tf_op jit(solution)/shard_map/ppermute | solution.py:50
  231.7 1.5 collective-permute-start.36
  234.3 1.1 collective-permute-done.36
  235.5 4.7 %subtract_reduce_fusion = f32[4096]{0:T(1024)S(1)} fusion(f32[2048,4096]{1,0:T(8,128)S(1)} %copy-done, f32[2048]{0:T(1024)S(1)} %multiply_subtract_fusion.4), kind=kLoop, calls=%fused_computation.7 | loop fusion | flops 16773120 | bytes 33579008 | tf_op jit(solution)/shard_map/reduce_max | solution.py:88
  240.2 7.6 %exponential_reduce_fusion = f32[4096]{0:T(1024)S(1)} fusion(f32[2048,4096]{1,0:T(8,128)S(1)} %copy-done, f32[4096]{0:T(1024)S(1)} %broadcast_divide_fusion, f32[2048]{0:T(1024)S(1)} %multiply_subtract_fusion.4, f32[]{:T(128)} %bitcast), kind=kLoop, calls=%fused_computation | loop fusion | flops 33550336 | bytes 33595396 | tf_op jit(solution)/shard_map/reduce_sum | solution.py:89
  248.0 2.7 collective-permute-start.38
  250.7 1.4 collective-permute-start.39
  253.5 1.1 collective-permute-done.39
  254.9 2.7 %collective-permute-start.41 = (f32[2,4096]{1,0:T(2,128)S(1)}, f32[2,4096]{1,0:T(2,128)S(1)}, u32[]{:S(2)}, u32[]{:S(2)}) collective-permute-start(f32[2,4096]{1,0:T(2,128)S(1)} %pad_maximum_fusion.8), channel_id=1, source_target_pairs={{0,64},{8,72},{16,80},{24,88},{32,96},{40,104},{48,112},{56,120},{... | collective-permute-start | bytes 98312 | tf_op jit(solution)/shard_map/ppermute | solution.py:50
  257.6 1.4 collective-permute-start.42
  260.4 1.1 collective-permute-done.42
  (119 shorter events, 21.1 us)
Async XLA Ops:
  7.2 30.6 %copy-start.1 = (f32[256,256]{1,0:T(8,128)S(1)}, f32[256,256]{1,0:T(8,128)}, u32[]{:S(2)}) copy-start(f32[256,256]{1,0:T(8,128)} %param.3) | copy-start | bytes 786436
  7.2 56.0 %all-gather.2.cloned.1.call-start = ((), (), s32[]{:S(2)}) async-start(), calls=%async_computation | async-start | bytes 3760128 | tf_op jit(solution)/shard_map/all_gather | solution.py:116
  9.7 8.1 %collective-permute-start.7 = (f32[40,256]{1,0:T(8,128)S(1)}, f32[40,256]{1,0:T(8,128)S(1)}, u32[]{:S(2)}, u32[]{:S(2)}) collective-permute-start(f32[40,256]{1,0:T(8,128)S(1)} %get-tuple-element.7), channel_id=1, source_target_pairs={{0,8},{8,16},{16,24},{24,0},{32,40},{40,48},{48,56},{56,32},{64,72... | collective-permute-start | bytes 122888 | tf_op jit(solution)/shard_map/ppermute | solution.py:35
  11.4 6.5 %collective-permute-start.8 = (f32[40,256]{1,0:T(8,128)S(1)}, f32[40,256]{1,0:T(8,128)S(1)}, u32[]{:S(2)}, u32[]{:S(2)}) collective-permute-start(f32[40,256]{1,0:T(8,128)S(1)} %get-tuple-element.7), channel_id=1, source_target_pairs={{0,16},{8,24},{16,0},{24,8},{32,48},{40,56},{48,32},{56,40},{64,80... | collective-permute-start | bytes 122888 | tf_op jit(solution)/shard_map/ppermute | solution.py:35
  14.3 4.0 %collective-permute-start.9 = (f32[40,256]{1,0:T(8,128)S(1)}, f32[40,256]{1,0:T(8,128)S(1)}, u32[]{:S(2)}, u32[]{:S(2)}) collective-permute-start(f32[40,256]{1,0:T(8,128)S(1)} %get-tuple-element.7), channel_id=1, source_target_pairs={{0,24},{8,0},{16,8},{24,16},{32,56},{40,32},{48,40},{56,48},{64,88... | collective-permute-start | bytes 122888 | tf_op jit(solution)/shard_map/ppermute | solution.py:35
  15.6 22.1 %collective-permute-start = (f32[256,256]{1,0:T(8,128)}, f32[256,256]{1,0:T(8,128)S(1)}, u32[]{:S(2)}, u32[]{:S(2)}) collective-permute-start(f32[256,256]{1,0:T(8,128)} %param.3), channel_id=1, source_target_pairs={{0,1},{1,2},{2,3},{3,4},{4,5},{5,6},{6,7},{7,0},{8,9},{9,10},{10,1... | collective-permute-start | bytes 786440 | tf_op jit(solution)/shard_map/ppermute | solution.py:35
  15.6 23.4 %collective-permute-start.1 = (f32[256,256]{1,0:T(8,128)}, f32[256,256]{1,0:T(8,128)S(1)}, u32[]{:S(2)}, u32[]{:S(2)}) collective-permute-start(f32[256,256]{1,0:T(8,128)} %param.3), channel_id=1, source_target_pairs={{0,2},{1,3},{2,4},{3,5},{4,6},{5,7},{6,0},{7,1},{8,10},{9,11},{10,... | collective-permute-start | bytes 786440 | tf_op jit(solution)/shard_map/ppermute | solution.py:35
  18.4 9.4 %collective-permute-start.10 = (f32[160,256]{1,0:T(8,128)S(1)}, f32[160,256]{1,0:T(8,128)S(1)}, u32[]{:S(2)}, u32[]{:S(2)}) collective-permute-start(f32[160,256]{1,0:T(8,128)S(1)} %get-tuple-element.9), channel_id=1, source_target_pairs={{0,32},{8,40},{16,48},{24,56},{32,64},{40,72},{48,80},{56,88},{64,... | collective-permute-start | bytes 491528 | tf_op jit(solution)/shard_map/ppermute | solution.py:35
  20.4 14.5 %collective-permute-start.11 = (f32[160,256]{1,0:T(8,128)S(1)}, f32[160,256]{1,0:T(8,128)S(1)}, u32[]{:S(2)}, u32[]{:S(2)}) collective-permute-start(f32[160,256]{1,0:T(8,128)S(1)} %get-tuple-element.9), channel_id=1, source_target_pairs={{0,64},{8,72},{16,80},{24,88},{32,96},{40,104},{48,112},{56,120},{... | collective-permute-start | bytes 491528 | tf_op jit(solution)/shard_map/ppermute | solution.py:35
  23.9 12.1 %collective-permute-start.12 = (f32[160,256]{1,0:T(8,128)S(1)}, f32[160,256]{1,0:T(8,128)S(1)}, u32[]{:S(2)}, u32[]{:S(2)}) collective-permute-start(f32[160,256]{1,0:T(8,128)S(1)} %get-tuple-element.9), channel_id=1, source_target_pairs={{0,96},{8,104},{16,112},{24,120},{32,0},{40,8},{48,16},{56,24},{64... | collective-permute-start | bytes 491528 | tf_op jit(solution)/shard_map/ppermute | solution.py:35
  27.8 12.0 %collective-permute-start.2 = (f32[256,256]{1,0:T(8,128)}, f32[256,256]{1,0:T(8,128)S(1)}, u32[]{:S(2)}, u32[]{:S(2)}) collective-permute-start(f32[256,256]{1,0:T(8,128)} %param.3), channel_id=1, source_target_pairs={{0,3},{1,4},{2,5},{3,6},{4,7},{5,0},{6,1},{7,2},{8,11},{9,12},{10,... | collective-permute-start | bytes 786440 | tf_op jit(solution)/shard_map/ppermute | solution.py:35
  34.8 10.0 %collective-permute-start.3 = (f32[256,256]{1,0:T(8,128)}, f32[256,256]{1,0:T(8,128)S(1)}, u32[]{:S(2)}, u32[]{:S(2)}) collective-permute-start(f32[256,256]{1,0:T(8,128)} %param.3), channel_id=1, source_target_pairs={{0,4},{1,5},{2,6},{3,7},{4,0},{5,1},{6,2},{7,3},{8,12},{9,13},{10,... | collective-permute-start | bytes 786440 | tf_op jit(solution)/shard_map/ppermute | solution.py:35
  36.1 9.5 %collective-permute-start.4 = (f32[256,256]{1,0:T(8,128)}, f32[256,256]{1,0:T(8,128)S(1)}, u32[]{:S(2)}, u32[]{:S(2)}) collective-permute-start(f32[256,256]{1,0:T(8,128)} %param.3), channel_id=1, source_target_pairs={{0,5},{1,6},{2,7},{3,0},{4,1},{5,2},{6,3},{7,4},{8,13},{9,14},{10,... | collective-permute-start | bytes 786440 | tf_op jit(solution)/shard_map/ppermute | solution.py:35
  37.8 15.7 %collective-permute-start.5 = (f32[256,256]{1,0:T(8,128)S(1)}, f32[256,256]{1,0:T(8,128)S(1)}, u32[]{:S(2)}, u32[]{:S(2)}) collective-permute-start(f32[256,256]{1,0:T(8,128)S(1)} %copy-done.1), channel_id=1, source_target_pairs={{0,6},{1,7},{2,0},{3,1},{4,2},{5,3},{6,4},{7,5},{8,14},{9,15},{10,... | collective-permute-start | bytes 786440 | tf_op jit(solution)/shard_map/ppermute | solution.py:35
  39.1 16.5 %collective-permute-start.6 = (f32[256,256]{1,0:T(8,128)S(1)}, f32[256,256]{1,0:T(8,128)S(1)}, u32[]{:S(2)}, u32[]{:S(2)}) collective-permute-start(f32[256,256]{1,0:T(8,128)S(1)} %copy-done.1), channel_id=1, source_target_pairs={{0,7},{1,0},{2,1},{3,2},{4,3},{5,4},{6,5},{7,6},{8,15},{9,8},{10,9... | collective-permute-start | bytes 786440 | tf_op jit(solution)/shard_map/ppermute | solution.py:35
  115.5 1.3 collective-permute-start.13
  116.9 5.7 %collective-permute-start.14 = (f32[2,2048]{1,0:T(2,128)S(1)}, f32[2,2048]{1,0:T(2,128)S(1)}, u32[]{:S(2)}, u32[]{:S(2)}) collective-permute-start(f32[2,2048]{1,0:T(2,128)S(1)} %pad_maximum_fusion.10), channel_id=1, source_target_pairs={{0,2},{1,3},{2,4},{3,5},{4,6},{5,7},{6,0},{7,1},{8,10},{9,11},{10,... | collective-permute-start | bytes 49160 | tf_op jit(solution)/shard_map/ppermute | solution.py:50
  118.4 5.2 %collective-permute-start.15 = (f32[2,2048]{1,0:T(2,128)S(1)}, f32[2,2048]{1,0:T(2,128)S(1)}, u32[]{:S(2)}, u32[]{:S(2)}) collective-permute-start(f32[2,2048]{1,0:T(2,128)S(1)} %pad_maximum_fusion.10), channel_id=1, source_target_pairs={{0,4},{1,5},{2,6},{3,7},{4,0},{5,1},{6,2},{7,3},{8,12},{9,13},{10,... | collective-permute-start | bytes 49160 | tf_op jit(solution)/shard_map/ppermute | solution.py:50
  121.1 3.7 %collective-permute-start.16 = (f32[2,2048]{1,0:T(2,128)S(1)}, f32[2,2048]{1,0:T(2,128)S(1)}, u32[]{:S(2)}, u32[]{:S(2)}) collective-permute-start(f32[2,2048]{1,0:T(2,128)S(1)} %pad_maximum_fusion.10), channel_id=1, source_target_pairs={{0,6},{1,7},{2,0},{3,1},{4,2},{5,3},{6,4},{7,5},{8,14},{9,15},{10,... | collective-permute-start | bytes 49160 | tf_op jit(solution)/shard_map/ppermute | solution.py:50
  124.9 20.2 %copy-start = (f32[2048,4096]{1,0:T(8,128)S(1)}, f32[2048,4096]{1,0:T(8,128)}, u32[]{:S(2)}) copy-start(f32[2048,4096]{1,0:T(8,128)} %get-tuple-element.59) | copy-start | bytes 100663296
  152.7 5.2 %collective-permute-start.17 = (f32[2,4096]{1,0:T(2,128)S(1)}, f32[2,4096]{1,0:T(2,128)S(1)}, u32[]{:S(2)}, u32[]{:S(2)}) collective-permute-start(f32[2,4096]{1,0:T(2,128)S(1)} %pad_maximum_fusion.3), channel_id=1, source_target_pairs={{0,8},{8,16},{16,24},{24,0},{32,40},{40,48},{48,56},{56,32},{64,72... | collective-permute-start | bytes 98312 | tf_op jit(solution)/shard_map/ppermute | solution.py:50
  153.5 5.4 %collective-permute-start.18 = (f32[2,4096]{1,0:T(2,128)S(1)}, f32[2,4096]{1,0:T(2,128)S(1)}, u32[]{:S(2)}, u32[]{:S(2)}) collective-permute-start(f32[2,4096]{1,0:T(2,128)S(1)} %pad_maximum_fusion.3), channel_id=1, source_target_pairs={{0,16},{8,24},{16,0},{24,8},{32,48},{40,56},{48,32},{56,40},{64,80... | collective-permute-start | bytes 98312 | tf_op jit(solution)/shard_map/ppermute | solution.py:50
  156.2 3.9 %collective-permute-start.19 = (f32[2,4096]{1,0:T(2,128)S(1)}, f32[2,4096]{1,0:T(2,128)S(1)}, u32[]{:S(2)}, u32[]{:S(2)}) collective-permute-start(f32[2,4096]{1,0:T(2,128)S(1)} %pad_maximum_fusion.3), channel_id=1, source_target_pairs={{0,24},{8,0},{16,8},{24,16},{32,56},{40,32},{48,40},{56,48},{64,88... | collective-permute-start | bytes 98312 | tf_op jit(solution)/shard_map/ppermute | solution.py:50
  160.3 5.2 %collective-permute-start.20 = (f32[2,4096]{1,0:T(2,128)S(1)}, f32[2,4096]{1,0:T(2,128)S(1)}, u32[]{:S(2)}, u32[]{:S(2)}) collective-permute-start(f32[2,4096]{1,0:T(2,128)S(1)} %pad_maximum_fusion.4), channel_id=1, source_target_pairs={{0,32},{8,40},{16,48},{24,56},{32,64},{40,72},{48,80},{56,88},{64,... | collective-permute-start | bytes 98312 | tf_op jit(solution)/shard_map/ppermute | solution.py:50
  160.5 5.4 %collective-permute-start.21 = (f32[2,4096]{1,0:T(2,128)S(1)}, f32[2,4096]{1,0:T(2,128)S(1)}, u32[]{:S(2)}, u32[]{:S(2)}) collective-permute-start(f32[2,4096]{1,0:T(2,128)S(1)} %pad_maximum_fusion.4), channel_id=1, source_target_pairs={{0,64},{8,72},{16,80},{24,88},{32,96},{40,104},{48,112},{56,120},{... | collective-permute-start | bytes 98312 | tf_op jit(solution)/shard_map/ppermute | solution.py:50
  163.1 3.9 %collective-permute-start.22 = (f32[2,4096]{1,0:T(2,128)S(1)}, f32[2,4096]{1,0:T(2,128)S(1)}, u32[]{:S(2)}, u32[]{:S(2)}) collective-permute-start(f32[2,4096]{1,0:T(2,128)S(1)} %pad_maximum_fusion.4), channel_id=1, source_target_pairs={{0,96},{8,104},{16,112},{24,120},{32,0},{40,8},{48,16},{56,24},{64... | collective-permute-start | bytes 98312 | tf_op jit(solution)/shard_map/ppermute | solution.py:50
  178.2 1.3 collective-permute-start.23
  179.6 5.0 %collective-permute-start.24 = (f32[2,2048]{1,0:T(2,128)S(1)}, f32[2,2048]{1,0:T(2,128)S(1)}, u32[]{:S(2)}, u32[]{:S(2)}) collective-permute-start(f32[2,2048]{1,0:T(2,128)S(1)} %pad_maximum_fusion.12), channel_id=1, source_target_pairs={{0,2},{1,3},{2,4},{3,5},{4,6},{5,7},{6,0},{7,1},{8,10},{9,11},{10,... | collective-permute-start | bytes 49160 | tf_op jit(solution)/shard_map/ppermute | solution.py:50
  180.0 5.7 %collective-permute-start.25 = (f32[2,2048]{1,0:T(2,128)S(1)}, f32[2,2048]{1,0:T(2,128)S(1)}, u32[]{:S(2)}, u32[]{:S(2)}) collective-permute-start(f32[2,2048]{1,0:T(2,128)S(1)} %pad_maximum_fusion.12), channel_id=1, source_target_pairs={{0,4},{1,5},{2,6},{3,7},{4,0},{5,1},{6,2},{7,3},{8,12},{9,13},{10,... | collective-permute-start | bytes 49160 | tf_op jit(solution)/shard_map/ppermute | solution.py:50
  183.8 3.7 %collective-permute-start.26 = (f32[2,2048]{1,0:T(2,128)S(1)}, f32[2,2048]{1,0:T(2,128)S(1)}, u32[]{:S(2)}, u32[]{:S(2)}) collective-permute-start(f32[2,2048]{1,0:T(2,128)S(1)} %pad_maximum_fusion.12), channel_id=1, source_target_pairs={{0,6},{1,7},{2,0},{3,1},{4,2},{5,3},{6,4},{7,5},{8,14},{9,15},{10,... | collective-permute-start | bytes 49160 | tf_op jit(solution)/shard_map/ppermute | solution.py:50
  200.0 5.2 %collective-permute-start.27 = (f32[2,4096]{1,0:T(2,128)S(1)}, f32[2,4096]{1,0:T(2,128)S(1)}, u32[]{:S(2)}, u32[]{:S(2)}) collective-permute-start(f32[2,4096]{1,0:T(2,128)S(1)} %pad_maximum_fusion.5), channel_id=1, source_target_pairs={{0,8},{8,16},{16,24},{24,0},{32,40},{40,48},{48,56},{56,32},{64,72... | collective-permute-start | bytes 98312 | tf_op jit(solution)/shard_map/ppermute | solution.py:50
  201.5 5.4 %collective-permute-start.28 = (f32[2,4096]{1,0:T(2,128)S(1)}, f32[2,4096]{1,0:T(2,128)S(1)}, u32[]{:S(2)}, u32[]{:S(2)}) collective-permute-start(f32[2,4096]{1,0:T(2,128)S(1)} %pad_maximum_fusion.5), channel_id=1, source_target_pairs={{0,16},{8,24},{16,0},{24,8},{32,48},{40,56},{48,32},{56,40},{64,80... | collective-permute-start | bytes 98312 | tf_op jit(solution)/shard_map/ppermute | solution.py:50
  204.2 3.9 %collective-permute-start.29 = (f32[2,4096]{1,0:T(2,128)S(1)}, f32[2,4096]{1,0:T(2,128)S(1)}, u32[]{:S(2)}, u32[]{:S(2)}) collective-permute-start(f32[2,4096]{1,0:T(2,128)S(1)} %pad_maximum_fusion.5), channel_id=1, source_target_pairs={{0,24},{8,0},{16,8},{24,16},{32,56},{40,32},{48,40},{56,48},{64,88... | collective-permute-start | bytes 98312 | tf_op jit(solution)/shard_map/ppermute | solution.py:50
  208.3 5.2 %collective-permute-start.30 = (f32[2,4096]{1,0:T(2,128)S(1)}, f32[2,4096]{1,0:T(2,128)S(1)}, u32[]{:S(2)}, u32[]{:S(2)}) collective-permute-start(f32[2,4096]{1,0:T(2,128)S(1)} %pad_maximum_fusion.6), channel_id=1, source_target_pairs={{0,32},{8,40},{16,48},{24,56},{32,64},{40,72},{48,80},{56,88},{64,... | collective-permute-start | bytes 98312 | tf_op jit(solution)/shard_map/ppermute | solution.py:50
  209.7 5.4 %collective-permute-start.31 = (f32[2,4096]{1,0:T(2,128)S(1)}, f32[2,4096]{1,0:T(2,128)S(1)}, u32[]{:S(2)}, u32[]{:S(2)}) collective-permute-start(f32[2,4096]{1,0:T(2,128)S(1)} %pad_maximum_fusion.6), channel_id=1, source_target_pairs={{0,64},{8,72},{16,80},{24,88},{32,96},{40,104},{48,112},{56,120},{... | collective-permute-start | bytes 98312 | tf_op jit(solution)/shard_map/ppermute | solution.py:50
  212.4 3.9 %collective-permute-start.32 = (f32[2,4096]{1,0:T(2,128)S(1)}, f32[2,4096]{1,0:T(2,128)S(1)}, u32[]{:S(2)}, u32[]{:S(2)}) collective-permute-start(f32[2,4096]{1,0:T(2,128)S(1)} %pad_maximum_fusion.6), channel_id=1, source_target_pairs={{0,96},{8,104},{16,112},{24,120},{32,0},{40,8},{48,16},{56,24},{64... | collective-permute-start | bytes 98312 | tf_op jit(solution)/shard_map/ppermute | solution.py:50
  227.6 1.3 collective-permute-start.33
  228.9 5.0 %collective-permute-start.34 = (f32[2,2048]{1,0:T(2,128)S(1)}, f32[2,2048]{1,0:T(2,128)S(1)}, u32[]{:S(2)}, u32[]{:S(2)}) collective-permute-start(f32[2,2048]{1,0:T(2,128)S(1)} %pad_maximum_fusion.14), channel_id=1, source_target_pairs={{0,2},{1,3},{2,4},{3,5},{4,6},{5,7},{6,0},{7,1},{8,10},{9,11},{10,... | collective-permute-start | bytes 49160 | tf_op jit(solution)/shard_map/ppermute | solution.py:50
  229.0 5.3 %collective-permute-start.35 = (f32[2,2048]{1,0:T(2,128)S(1)}, f32[2,2048]{1,0:T(2,128)S(1)}, u32[]{:S(2)}, u32[]{:S(2)}) collective-permute-start(f32[2,2048]{1,0:T(2,128)S(1)} %pad_maximum_fusion.14), channel_id=1, source_target_pairs={{0,4},{1,5},{2,6},{3,7},{4,0},{5,1},{6,2},{7,3},{8,12},{9,13},{10,... | collective-permute-start | bytes 49160 | tf_op jit(solution)/shard_map/ppermute | solution.py:50
  231.7 3.7 %collective-permute-start.36 = (f32[2,2048]{1,0:T(2,128)S(1)}, f32[2,2048]{1,0:T(2,128)S(1)}, u32[]{:S(2)}, u32[]{:S(2)}) collective-permute-start(f32[2,2048]{1,0:T(2,128)S(1)} %pad_maximum_fusion.14), channel_id=1, source_target_pairs={{0,6},{1,7},{2,0},{3,1},{4,2},{5,3},{6,4},{7,5},{8,14},{9,15},{10,... | collective-permute-start | bytes 49160 | tf_op jit(solution)/shard_map/ppermute | solution.py:50
  235.5 4.8 %copy-start.2 = (f32[2048]{0:T(1024)}, f32[2048]{0:T(1024)S(1)}, u32[]{:S(2)}) copy-start(f32[2048]{0:T(1024)S(1)} %multiply_subtract_fusion.4) | copy-start | bytes 24580
  247.9 5.2 %collective-permute-start.37 = (f32[2,4096]{1,0:T(2,128)S(1)}, f32[2,4096]{1,0:T(2,128)S(1)}, u32[]{:S(2)}, u32[]{:S(2)}) collective-permute-start(f32[2,4096]{1,0:T(2,128)S(1)} %pad_maximum_fusion.7), channel_id=1, source_target_pairs={{0,8},{8,16},{16,24},{24,0},{32,40},{40,48},{48,56},{56,32},{64,72... | collective-permute-start | bytes 98312 | tf_op jit(solution)/shard_map/ppermute | solution.py:50
  248.0 5.5 %collective-permute-start.38 = (f32[2,4096]{1,0:T(2,128)S(1)}, f32[2,4096]{1,0:T(2,128)S(1)}, u32[]{:S(2)}, u32[]{:S(2)}) collective-permute-start(f32[2,4096]{1,0:T(2,128)S(1)} %pad_maximum_fusion.7), channel_id=1, source_target_pairs={{0,16},{8,24},{16,0},{24,8},{32,48},{40,56},{48,32},{56,40},{64,80... | collective-permute-start | bytes 98312 | tf_op jit(solution)/shard_map/ppermute | solution.py:50
  250.7 3.9 %collective-permute-start.39 = (f32[2,4096]{1,0:T(2,128)S(1)}, f32[2,4096]{1,0:T(2,128)S(1)}, u32[]{:S(2)}, u32[]{:S(2)}) collective-permute-start(f32[2,4096]{1,0:T(2,128)S(1)} %pad_maximum_fusion.7), channel_id=1, source_target_pairs={{0,24},{8,0},{16,8},{24,16},{32,56},{40,32},{48,40},{56,48},{64,88... | collective-permute-start | bytes 98312 | tf_op jit(solution)/shard_map/ppermute | solution.py:50
  254.8 5.2 %collective-permute-start.40 = (f32[2,4096]{1,0:T(2,128)S(1)}, f32[2,4096]{1,0:T(2,128)S(1)}, u32[]{:S(2)}, u32[]{:S(2)}) collective-permute-start(f32[2,4096]{1,0:T(2,128)S(1)} %pad_maximum_fusion.8), channel_id=1, source_target_pairs={{0,32},{8,40},{16,48},{24,56},{32,64},{40,72},{48,80},{56,88},{64,... | collective-permute-start | bytes 98312 | tf_op jit(solution)/shard_map/ppermute | solution.py:50
  254.9 5.5 %collective-permute-start.41 = (f32[2,4096]{1,0:T(2,128)S(1)}, f32[2,4096]{1,0:T(2,128)S(1)}, u32[]{:S(2)}, u32[]{:S(2)}) collective-permute-start(f32[2,4096]{1,0:T(2,128)S(1)} %pad_maximum_fusion.8), channel_id=1, source_target_pairs={{0,64},{8,72},{16,80},{24,88},{32,96},{40,104},{48,112},{56,120},{... | collective-permute-start | bytes 98312 | tf_op jit(solution)/shard_map/ppermute | solution.py:50
  257.6 3.9 %collective-permute-start.42 = (f32[2,4096]{1,0:T(2,128)S(1)}, f32[2,4096]{1,0:T(2,128)S(1)}, u32[]{:S(2)}, u32[]{:S(2)}) collective-permute-start(f32[2,4096]{1,0:T(2,128)S(1)} %pad_maximum_fusion.8), channel_id=1, source_target_pairs={{0,96},{8,104},{16,112},{24,120},{32,0},{40,8},{48,16},{56,24},{64... | collective-permute-start | bytes 98312 | tf_op jit(solution)/shard_map/ppermute | solution.py:50
Sparse Core Ops, SparseCore 0:
  10.1 53.0 all-gather.1
where the time goes:
time: 270 us; the launch traced here: 269 us
  other arithmetic  85.2 us (32%)
  starting transfers between devices  60.7 us (22%)
  waiting for transfers between devices  59.9 us (22%)
  matrix products  34.8 us (13%)
  between operations  15.3 us (6%)
  local copies, waits for them, and re-layouts  13.4 us (5%)
    ppermute x30, starting transfers between devices, combine_over(): lax.ppermute(packed, axis, digit_partners(axis, size, stride, width, k))  40.3 us
    dot_general x1, matrix products, inner_costs(): lax.dot_general(left, right, (((1,), (1,)), ((), ())), precision=lax.Prec...  34.8 us
    reduce_sum x3, other arithmetic, logsum_col(): totals = jnp.sum(jnp.exp(gaps / scale - peak[:, None]), axis=1)  30.6 us
    ppermute x30, waiting for transfers between devices, combine_over(): lax.ppermute(packed, axis, digit_partners(axis, size, stride, width, k))  29.3 us
    ppermute x13, waiting for transfers between devices, exchange(): lax.ppermute(x, axis, digit_partners(axis, size, stride, width, k))  23.6 us
    reduce_max x3, other arithmetic, logsum_row(): peak = jnp.max(gaps, axis=0) / scale  23.2 us
    reduce_sum x3, other arithmetic, logsum_row(): totals = jnp.sum(jnp.exp(gaps / scale - peak[None, :]), axis=0)  22.9 us
    ppermute x13, starting transfers between devices, exchange(): lax.ppermute(x, axis, digit_partners(axis, size, stride, width, k))  20.3 us
  transfers between devices with their start and end apart: 44, of which 37 were waited for; matrix products, arithmetic and copies ran while one was open for 1% of the time, Pallas kernels for 0%

commit v1 on v0

--- a/solution.py
+++ b/solution.py
@@ -5,6 +5,12 @@
 from jax.sharding import PartitionSpec as P
 
 ITERS = 3
+
+
+def place_the_stages_all(base_x):
+    n = lax.axis_size("row")
+    r_now = jnp.tile(base_x, [n if dd == 0 else 1 for dd in range(base_x.ndim)])
+    return lax.all_to_all(r_now, "row", split_axis=0, concat_axis=0, tiled=True)
 
 
 def inner_costs(left, right):
@@ -113,8 +119,7 @@
     rows = passages.shape[0]
     split = rows - rows * 5 // 32
     passage_block = jnp.concatenate(
-        [lax.all_gather(passages[:split], "row", axis=0, tiled=True), gather_row(passages[split:])],
-        axis=0,
+        [place_the_stages_all(passages[:split]), gather_row(passages[split:])], axis=0
     )
     cost_tile = inner_costs(query_block, passage_block)
     col_potential = jnp.zeros((cost_tile.shape[1],), jnp.float32)

time: 270 us -> 296 us (1.096)
  waiting for transfers between devices: 59.9 us -> 77.5 us
  starting transfers between devices: 60.7 us -> 74.9 us
  between operations: 15.3 us -> 2.27 us
  local copies, waits for them, and re-layouts: 13.4 us -> 18.3 us
    ppermute x13, waiting for transfers between devices: 23.6 us -> 49.1 us  [exchange(): lax.ppermute(x, axis, digit_partners(axis, size, stride, width, k))]
    ppermute x30, starting transfers between devices: 40.3 us -> 49.4 us  [combine_over(): lax.ppermute(packed, axis, digit_partners(axis, size, stride, width, k))]
    all_gather x1 -> x0, waiting for transfers between devices: 6.99 us -> none  [per_device(): lax.all_gather(passages[:split], 'row', axis=0, tiled=True)]
    all_to_all x0 -> x1, starting transfers between devices: none -> 5.53 us  [place_the_stages_all(): return lax.all_to_all(r_now, 'row', split_axis=0, concat_axis=0, tiled=True)]
    unnamed x25 -> x29, local copies, waits for them, and re-layouts: 10.5 us -> 13.5 us
  transfers between devices with their start and end apart: 44 -> 44, of which waited for: 37 -> 34; matrix products, arithmetic and copies ran while one was open for 1% -> 3% of each run, Pallas kernels for 0% -> 0%
where the time goes in v1:
time: 296 us; the launch traced here: 295 us
  other arithmetic  87.3 us (29%)
  waiting for transfers between devices  77.5 us (26%)
  starting transfers between devices  74.9 us (25%)
  matrix products  34.8 us (12%)
  local copies, waits for them, and re-layouts  18.3 us (6%)
    ppermute x30, starting transfers between devices, combine_over(): lax.ppermute(packed, axis, digit_partners(axis, size, stride, width, k))  49.4 us
    ppermute x13, waiting for transfers between devices, exchange(): lax.ppermute(x, axis, digit_partners(axis, size, stride, width, k))  49.1 us
    dot_general x1, matrix products, inner_costs(): lax.dot_general(left, right, (((1,), (1,)), ((), ())), precision=lax.Prec...  34.8 us
    reduce_sum x3, other arithmetic, logsum_col(): totals = jnp.sum(jnp.exp(gaps / scale - peak[:, None]), axis=1)  31 us
    ppermute x30, waiting for transfers between devices, combine_over(): lax.ppermute(packed, axis, digit_partners(axis, size, stride, width, k))  28.3 us
    reduce_max x3, other arithmetic, logsum_row(): peak = jnp.max(gaps, axis=0) / scale  23.2 us
    reduce_sum x3, other arithmetic, logsum_row(): totals = jnp.sum(jnp.exp(gaps / scale - peak[None, :]), axis=0)  22.9 us
    ppermute x13, starting transfers between devices, exchange(): lax.ppermute(x, axis, digit_partners(axis, size, stride, width, k))  19.9 us
  transfers between devices with their start and end apart: 44, of which 34 were waited for; matrix products, arithmetic and copies ran while one was open for 3% of the time, Pallas kernels for 0%

profile of v1, /device:TPU:0, one launch (start us, length us, event | category | flops | bytes accessed | tf_op | source)
XLA Modules:
  0.0 295.0 jit_solution(11168883306346945445)
XLA Ops:
  0.6 1.4 slice_bitcast_fusion
  2.0 1.7 collective-permute-start.7
  3.7 2.9 collective-permute-start.8
  6.6 1.3 collective-permute-start.9
  8.0 1.5 collective-permute-start.1
  10.4 2.0 tile.2
  12.4 5.5 %all-to-all-start = ((f32[16,216,256]{2,1,0:T(8,128)}), f32[16,216,256]{2,1,0:T(8,128)S(1)}, u32[]{:S(2)}, u32[]{:S(2)}) async-start(f32[16,216,256]{2,1,0:T(8,128)} %tile.2), calls=%async_computation | async-start | bytes 7077888 | tf_op jit(solution)/shard_map/all_to_all | solution.py:13
  19.9 1.7 collective-permute-start.10
  21.6 2.7 collective-permute-start.11
  24.3 1.5 collective-permute-start.12
  26.7 32.7 %collective-permute-done.10 = f32[160,256]{1,0:T(8,128)S(1)} collective-permute-done((f32[160,256]{1,0:T(8,128)S(1)}, f32[160,256]{1,0:T(8,128)S(1)}, u32[]{:S(2)}, u32[]{:S(2)}) %collective-permute-start.10) | collective-permute-done | bytes 163872 | tf_op jit(solution)/shard_map/ppermute | solution.py:41
  60.3 3.0 %collective-permute-done.11 = f32[160,256]{1,0:T(8,128)S(1)} collective-permute-done((f32[160,256]{1,0:T(8,128)S(1)}, f32[160,256]{1,0:T(8,128)S(1)}, u32[]{:S(2)}, u32[]{:S(2)}) %collective-permute-start.11) | collective-permute-done | bytes 163872 | tf_op jit(solution)/shard_map/ppermute | solution.py:41
  63.3 2.3 collective-permute-start.3
  68.1 2.9 collective-permute-start.5
  73.0 2.4 collective-permute-done.3
  75.4 1.7 collective-permute-done.4
  77.2 6.5 %collective-permute-done.5 = f32[256,256]{1,0:T(8,128)S(1)} collective-permute-done((f32[256,256]{1,0:T(8,128)}, f32[256,256]{1,0:T(8,128)S(1)}, u32[]{:S(2)}, u32[]{:S(2)}) %collective-permute-start.5) | collective-permute-done | bytes 262176 | tf_op jit(solution)/shard_map/ppermute | solution.py:41
  83.6 1.9 collective-permute-done.6
  85.8 1.3 copy-done.1
  90.2 34.8 %subtract_reduce_fusion.5 = (f32[2048]{0:T(1024)S(1)}, f32[2048,4096]{1,0:T(8,128)}) fusion(f32[2048,256]{1,0:T(8,128)S(1)} %copy-done.2, f32[4096,256]{1,0:T(8,128)S(1)} %bitcast_dynamic-update-slice_fusion.16, f32[4096]{0:T(1024)S(1)} %multiply_reduce_fusion, f32[2048]{0:T(1024)S(1)} %multiply_reduce_fusion.1), kind=kOutput, calls=%fused_computation.12 | convolution fusion | flops 25811744768 | bytes 39878656 | tf_op jit(solution)/shard_map/dot_general | solution.py:19
  125.0 14.5 %exponential_reduce_fusion.5 = f32[2048]{0:T(1024)S(1)} fusion(f32[2048,4096]{1,0:T(8,128)} %get-tuple-element.59, f32[2048]{0:T(1024)S(1)} %broadcast_divide_fusion.5, f32[]{:T(128)} %bitcast), kind=kLoop, calls=%fused_computation.5 | loop fusion | flops 33552384 | bytes 33570820 | tf_op jit(solution)/shard_map/reduce_sum | solution.py:89
  141.3 2.1 collective-permute-start.14
  143.4 2.1 collective-permute-start.15
  145.5 1.2 collective-permute-start.16
  146.7 1.9 collective-permute-done.15
  149.3 13.8 %subtract_reduce_fusion.4 = f32[4096]{0:T(1024)S(1)} fusion(f32[2048,4096]{1,0:T(8,128)} %get-tuple-element.59, f32[2048]{0:T(1024)S(1)} %multiply_subtract_fusion.6), kind=kLoop, calls=%fused_computation.11 | loop fusion | flops 16773120 | bytes 33579008 | tf_op jit(solution)/shard_map/reduce_max | solution.py:94
  163.1 6.3 %copy-done = f32[2048,4096]{1,0:T(8,128)S(1)} copy-done((f32[2048,4096]{1,0:T(8,128)S(1)}, f32[2048,4096]{1,0:T(8,128)}, u32[]{:S(2)}) %copy-start) | copy-done | bytes 33554456
  169.5 7.6 %exponential_reduce_fusion.4 = f32[4096]{0:T(1024)S(1)} fusion(f32[2048,4096]{1,0:T(8,128)S(1)} %copy-done, f32[4096]{0:T(1024)S(1)} %broadcast_divide_fusion.2, f32[2048]{0:T(1024)S(1)} %multiply_subtract_fusion.6, f32[]{:T(128)} %bitcast), kind=kLoop, calls=%fused_computation.4 | loop fusion | flops 33550336 | bytes 33595396 | tf_op jit(solution)/shard_map/reduce_sum | solution.py:95
  177.1 3.4 %collective-permute-start.17 = (f32[2,4096]{1,0:T(2,128)S(1)}, f32[2,4096]{1,0:T(2,128)S(1)}, u32[]{:S(2)}, u32[]{:S(2)}) collective-permute-start(f32[2,4096]{1,0:T(2,128)S(1)} %pad_maximum_fusion.3), channel_id=1, source_target_pairs={{0,8},{8,16},{16,24},{24,0},{32,40},{40,48},{48,56},{56,32},{64,72... | collective-permute-start | bytes 98312 | tf_op jit(solution)/shard_map/ppermute | solution.py:56
  180.5 5.7 %collective-permute-start.18 = (f32[2,4096]{1,0:T(2,128)S(1)}, f32[2,4096]{1,0:T(2,128)S(1)}, u32[]{:S(2)}, u32[]{:S(2)}) collective-permute-start(f32[2,4096]{1,0:T(2,128)S(1)} %pad_maximum_fusion.3), channel_id=1, source_target_pairs={{0,16},{8,24},{16,0},{24,8},{32,48},{40,56},{48,32},{56,40},{64,80... | collective-permute-start | bytes 98312 | tf_op jit(solution)/shard_map/ppermute | solution.py:56
  186.2 1.5 collective-permute-start.19
  188.4 1.7 collective-permute-done.19
  190.4 2.8 collective-permute-start.21
  193.2 2.5 collective-permute-start.22
  195.9 1.5 collective-permute-done.22
  197.5 3.0 %subtract_reduce_fusion.3 = f32[2048]{0:T(1024)S(1)} fusion(f32[2048,4096]{1,0:T(8,128)S(1)} %copy-done, f32[4096]{0:T(1024)S(1)} %bitcast.128), kind=kLoop, calls=%fused_computation.10 | loop fusion | flops 16775168 | bytes 33579008 | tf_op jit(solution)/shard_map/reduce_max | solution.py:88
  200.5 8.2 %exponential_reduce_fusion.3 = f32[2048]{0:T(1024)S(1)} fusion(f32[2048,4096]{1,0:T(8,128)S(1)} %copy-done, f32[2048]{0:T(1024)S(1)} %broadcast_divide_fusion.4, f32[4096]{0:T(1024)S(1)} %bitcast.129, f32[]{:T(128)} %bitcast), kind=kLoop, calls=%fused_computation.3 | loop fusion | flops 33552384 | bytes 33587204 | tf_op jit(solution)/shard_map/reduce_sum | solution.py:89
  208.8 1.2 collective-permute-done.23
  210.4 3.8 %collective-permute-start.25 = (f32[2,2048]{1,0:T(2,128)S(1)}, f32[2,2048]{1,0:T(2,128)S(1)}, u32[]{:S(2)}, u32[]{:S(2)}) collective-permute-start(f32[2,2048]{1,0:T(2,128)S(1)} %pad_maximum_fusion.12), channel_id=1, source_target_pairs={{0,4},{1,5},{2,6},{3,7},{4,0},{5,1},{6,2},{7,3},{8,12},{9,13},{10,... | collective-permute-start | bytes 49160 | tf_op jit(solution)/shard_map/ppermute | solution.py:56
  216.1 1.8 collective-permute-done.26
  218.0 4.7 %subtract_reduce_fusion.2 = f32[4096]{0:T(1024)S(1)} fusion(f32[2048,4096]{1,0:T(8,128)S(1)} %copy-done, f32[2048]{0:T(1024)S(1)} %multiply_subtract_fusion.5), kind=kLoop, calls=%fused_computation.9 | loop fusion | flops 16773120 | bytes 33579008 | tf_op jit(solution)/shard_map/reduce_max | solution.py:94
  222.7 7.6 %exponential_reduce_fusion.2 = f32[4096]{0:T(1024)S(1)} fusion(f32[2048,4096]{1,0:T(8,128)S(1)} %copy-done, f32[4096]{0:T(1024)S(1)} %broadcast_divide_fusion.1, f32[2048]{0:T(1024)S(1)} %multiply_subtract_fusion.5, f32[]{:T(128)} %bitcast), kind=kLoop, calls=%fused_computation.2 | loop fusion | flops 33550336 | bytes 33595396 | tf_op jit(solution)/shard_map/reduce_sum | solution.py:95
  230.4 1.2 collective-permute-start.27
  231.6 3.8 %collective-permute-start.28 = (f32[2,4096]{1,0:T(2,128)S(1)}, f32[2,4096]{1,0:T(2,128)S(1)}, u32[]{:S(2)}, u32[]{:S(2)}) collective-permute-start(f32[2,4096]{1,0:T(2,128)S(1)} %pad_maximum_fusion.5), channel_id=1, source_target_pairs={{0,16},{8,24},{16,0},{24,8},{32,48},{40,56},{48,32},{56,40},{64,80... | collective-permute-start | bytes 98312 | tf_op jit(solution)/shard_map/ppermute | solution.py:56
  235.9 1.8 collective-permute-done.28
  237.7 1.7 collective-permute-done.29
  239.5 1.2 collective-permute-start.30
  240.8 3.8 %collective-permute-start.31 = (f32[2,4096]{1,0:T(2,128)S(1)}, f32[2,4096]{1,0:T(2,128)S(1)}, u32[]{:S(2)}, u32[]{:S(2)}) collective-permute-start(f32[2,4096]{1,0:T(2,128)S(1)} %pad_maximum_fusion.6), channel_id=1, source_target_pairs={{0,64},{8,72},{16,80},{24,88},{32,96},{40,104},{48,112},{56,120},{... | collective-permute-start | bytes 98312 | tf_op jit(solution)/shard_map/ppermute | solution.py:56
  245.0 1.8 collective-permute-done.31
  246.8 1.7 collective-permute-done.32
  248.7 3.0 %subtract_reduce_fusion.1 = f32[2048]{0:T(1024)S(1)} fusion(f32[2048,4096]{1,0:T(8,128)S(1)} %copy-done, f32[4096]{0:T(1024)S(1)} %bitcast.130), kind=kLoop, calls=%fused_computation.8 | loop fusion | flops 16775168 | bytes 33579008 | tf_op jit(solution)/shard_map/reduce_max | solution.py:88
  251.7 8.2 %exponential_reduce_fusion.1 = f32[2048]{0:T(1024)S(1)} fusion(f32[2048,4096]{1,0:T(8,128)S(1)} %copy-done, f32[2048]{0:T(1024)S(1)} %broadcast_divide_fusion.3, f32[4096]{0:T(1024)S(1)} %bitcast.131, f32[]{:T(128)} %bitcast), kind=kLoop, calls=%fused_computation.1 | loop fusion | flops 33552384 | bytes 33587204 | tf_op jit(solution)/shard_map/reduce_sum | solution.py:89
  260.0 1.2 collective-permute-done.33
  261.4 2.8 collective-permute-start.35
  264.2 1.3 collective-permute-start.36
  266.7 1.3 collective-permute-done.36
  268.0 4.7 %subtract_reduce_fusion = f32[4096]{0:T(1024)S(1)} fusion(f32[2048,4096]{1,0:T(8,128)S(1)} %copy-done, f32[2048]{0:T(1024)S(1)} %multiply_subtract_fusion.4), kind=kLoop, calls=%fused_computation.7 | loop fusion | flops 16773120 | bytes 33579008 | tf_op jit(solution)/shard_map/reduce_max | solution.py:94
  272.8 7.6 %exponential_reduce_fusion = f32[4096]{0:T(1024)S(1)} fusion(f32[2048,4096]{1,0:T(8,128)S(1)} %copy-done, f32[4096]{0:T(1024)S(1)} %broadcast_divide_fusion, f32[2048]{0:T(1024)S(1)} %multiply_subtract_fusion.4, f32[]{:T(128)} %bitcast), kind=kLoop, calls=%fused_computation | loop fusion | flops 33550336 | bytes 33595396 | tf_op jit(solution)/shard_map/reduce_sum | solution.py:95
  280.6 2.7 collective-permute-start.38
  283.2 1.5 collective-permute-start.39
  286.1 1.1 collective-permute-done.39
  287.4 2.7 collective-permute-start.41
  290.1 1.5 collective-permute-start.42
  292.9 1.0 collective-permute-done.42
  (123 shorter events, 24.6 us)
Async XLA Ops:
  2.0 16.9 %collective-permute-start.7 = (f32[40,256]{1,0:T(8,128)}, f32[40,256]{1,0:T(8,128)}, u32[]{:S(2)}, u32[]{:S(2)}) collective-permute-start(f32[40,256]{1,0:T(8,128)} %get-tuple-element.7), channel_id=1, source_target_pairs={{0,8},{8,16},{16,24},{24,0},{32,40},{40,48},{48,56},{56,32},{64,72... | collective-permute-start | bytes 122888 | tf_op jit(solution)/shard_map/ppermute | solution.py:41
  3.7 15.3 %collective-permute-start.8 = (f32[40,256]{1,0:T(8,128)}, f32[40,256]{1,0:T(8,128)}, u32[]{:S(2)}, u32[]{:S(2)}) collective-permute-start(f32[40,256]{1,0:T(8,128)} %get-tuple-element.7), channel_id=1, source_target_pairs={{0,16},{8,24},{16,0},{24,8},{32,48},{40,56},{48,32},{56,40},{64,80... | collective-permute-start | bytes 122888 | tf_op jit(solution)/shard_map/ppermute | solution.py:41
  6.6 12.4 %collective-permute-start.9 = (f32[40,256]{1,0:T(8,128)}, f32[40,256]{1,0:T(8,128)}, u32[]{:S(2)}, u32[]{:S(2)}) collective-permute-start(f32[40,256]{1,0:T(8,128)} %get-tuple-element.7), channel_id=1, source_target_pairs={{0,24},{8,0},{16,8},{24,16},{32,56},{40,32},{48,40},{56,48},{64,88... | collective-permute-start | bytes 122888 | tf_op jit(solution)/shard_map/ppermute | solution.py:41
  8.0 60.1 %collective-permute-start = (f32[256,256]{1,0:T(8,128)}, f32[256,256]{1,0:T(8,128)}, u32[]{:S(2)}, u32[]{:S(2)}) collective-permute-start(f32[256,256]{1,0:T(8,128)} %param.3), channel_id=1, source_target_pairs={{0,1},{1,2},{2,3},{3,4},{4,5},{5,6},{6,7},{7,0},{8,9},{9,10},{10,1... | collective-permute-start | bytes 786440 | tf_op jit(solution)/shard_map/ppermute | solution.py:41
  8.0 64.0 %collective-permute-start.1 = (f32[256,256]{1,0:T(8,128)}, f32[256,256]{1,0:T(8,128)}, u32[]{:S(2)}, u32[]{:S(2)}) collective-permute-start(f32[256,256]{1,0:T(8,128)} %param.3), channel_id=1, source_target_pairs={{0,2},{1,3},{2,4},{3,5},{4,6},{5,7},{6,0},{7,1},{8,10},{9,11},{10,... | collective-permute-start | bytes 786440 | tf_op jit(solution)/shard_map/ppermute | solution.py:41
  12.4 75.1 %all-to-all-start = ((f32[16,216,256]{2,1,0:T(8,128)}), f32[16,216,256]{2,1,0:T(8,128)S(1)}, u32[]{:S(2)}, u32[]{:S(2)}) async-start(f32[16,216,256]{2,1,0:T(8,128)} %tile.2), calls=%async_computation | async-start | bytes 7077888 | tf_op jit(solution)/shard_map/all_to_all | solution.py:13
  19.9 39.5 %collective-permute-start.10 = (f32[160,256]{1,0:T(8,128)S(1)}, f32[160,256]{1,0:T(8,128)S(1)}, u32[]{:S(2)}, u32[]{:S(2)}) collective-permute-start(f32[160,256]{1,0:T(8,128)S(1)} %get-tuple-element.9), channel_id=1, source_target_pairs={{0,32},{8,40},{16,48},{24,56},{32,64},{40,72},{48,80},{56,88},{64,... | collective-permute-start | bytes 491528 | tf_op jit(solution)/shard_map/ppermute | solution.py:41
  21.6 41.6 %collective-permute-start.11 = (f32[160,256]{1,0:T(8,128)S(1)}, f32[160,256]{1,0:T(8,128)S(1)}, u32[]{:S(2)}, u32[]{:S(2)}) collective-permute-start(f32[160,256]{1,0:T(8,128)S(1)} %get-tuple-element.9), channel_id=1, source_target_pairs={{0,64},{8,72},{16,80},{24,88},{32,96},{40,104},{48,112},{56,120},{... | collective-permute-start | bytes 491528 | tf_op jit(solution)/shard_map/ppermute | solution.py:41
  24.3 42.3 %collective-permute-start.12 = (f32[160,256]{1,0:T(8,128)S(1)}, f32[160,256]{1,0:T(8,128)S(1)}, u32[]{:S(2)}, u32[]{:S(2)}) collective-permute-start(f32[160,256]{1,0:T(8,128)S(1)} %get-tuple-element.9), channel_id=1, source_target_pairs={{0,96},{8,104},{16,112},{24,120},{32,0},{40,8},{48,16},{56,24},{64... | collective-permute-start | bytes 491528 | tf_op jit(solution)/shard_map/ppermute | solution.py:41
  59.5 13.5 %collective-permute-start.2 = (f32[256,256]{1,0:T(8,128)}, f32[256,256]{1,0:T(8,128)S(1)}, u32[]{:S(2)}, u32[]{:S(2)}) collective-permute-start(f32[256,256]{1,0:T(8,128)} %param.3), channel_id=1, source_target_pairs={{0,3},{1,4},{2,5},{3,6},{4,7},{5,0},{6,1},{7,2},{8,11},{9,12},{10,... | collective-permute-start | bytes 786440 | tf_op jit(solution)/shard_map/ppermute | solution.py:41
  63.3 12.1 %collective-permute-start.3 = (f32[256,256]{1,0:T(8,128)}, f32[256,256]{1,0:T(8,128)S(1)}, u32[]{:S(2)}, u32[]{:S(2)}) collective-permute-start(f32[256,256]{1,0:T(8,128)} %param.3), channel_id=1, source_target_pairs={{0,4},{1,5},{2,6},{3,7},{4,0},{5,1},{6,2},{7,3},{8,12},{9,13},{10,... | collective-permute-start | bytes 786440 | tf_op jit(solution)/shard_map/ppermute | solution.py:41
  66.6 10.5 %collective-permute-start.4 = (f32[256,256]{1,0:T(8,128)}, f32[256,256]{1,0:T(8,128)S(1)}, u32[]{:S(2)}, u32[]{:S(2)}) collective-permute-start(f32[256,256]{1,0:T(8,128)} %param.3), channel_id=1, source_target_pairs={{0,5},{1,6},{2,7},{3,0},{4,1},{5,2},{6,3},{7,4},{8,13},{9,14},{10,... | collective-permute-start | bytes 786440 | tf_op jit(solution)/shard_map/ppermute | solution.py:41
  68.1 15.5 %collective-permute-start.5 = (f32[256,256]{1,0:T(8,128)}, f32[256,256]{1,0:T(8,128)S(1)}, u32[]{:S(2)}, u32[]{:S(2)}) collective-permute-start(f32[256,256]{1,0:T(8,128)} %param.3), channel_id=1, source_target_pairs={{0,6},{1,7},{2,0},{3,1},{4,2},{5,3},{6,4},{7,5},{8,14},{9,15},{10,... | collective-permute-start | bytes 786440 | tf_op jit(solution)/shard_map/ppermute | solution.py:41
  72.0 13.5 %collective-permute-start.6 = (f32[256,256]{1,0:T(8,128)}, f32[256,256]{1,0:T(8,128)S(1)}, u32[]{:S(2)}, u32[]{:S(2)}) collective-permute-start(f32[256,256]{1,0:T(8,128)} %param.3), channel_id=1, source_target_pairs={{0,7},{1,0},{2,1},{3,2},{4,3},{5,4},{6,5},{7,6},{8,15},{9,8},{10,9... | collective-permute-start | bytes 786440 | tf_op jit(solution)/shard_map/ppermute | solution.py:41
  85.8 1.3 copy-start.1
  87.5 1.1 copy-start.3
  88.6 1.6 copy-start.2
  139.6 1.7 collective-permute-start.13
  141.3 5.4 %collective-permute-start.14 = (f32[2,2048]{1,0:T(2,128)S(1)}, f32[2,2048]{1,0:T(2,128)S(1)}, u32[]{:S(2)}, u32[]{:S(2)}) collective-permute-start(f32[2,2048]{1,0:T(2,128)S(1)} %pad_maximum_fusion.10), channel_id=1, source_target_pairs={{0,2},{1,3},{2,4},{3,5},{4,6},{5,7},{6,0},{7,1},{8,10},{9,11},{10,... | collective-permute-start | bytes 49160 | tf_op jit(solution)/shard_map/ppermute | solution.py:56
  143.4 5.2 %collective-permute-start.15 = (f32[2,2048]{1,0:T(2,128)S(1)}, f32[2,2048]{1,0:T(2,128)S(1)}, u32[]{:S(2)}, u32[]{:S(2)}) collective-permute-start(f32[2,2048]{1,0:T(2,128)S(1)} %pad_maximum_fusion.10), channel_id=1, source_target_pairs={{0,4},{1,5},{2,6},{3,7},{4,0},{5,1},{6,2},{7,3},{8,12},{9,13},{10,... | collective-permute-start | bytes 49160 | tf_op jit(solution)/shard_map/ppermute | solution.py:56
  145.5 3.7 %collective-permute-start.16 = (f32[2,2048]{1,0:T(2,128)S(1)}, f32[2,2048]{1,0:T(2,128)S(1)}, u32[]{:S(2)}, u32[]{:S(2)}) collective-permute-start(f32[2,2048]{1,0:T(2,128)S(1)} %pad_maximum_fusion.10), channel_id=1, source_target_pairs={{0,6},{1,7},{2,0},{3,1},{4,2},{5,3},{6,4},{7,5},{8,14},{9,15},{10,... | collective-permute-start | bytes 49160 | tf_op jit(solution)/shard_map/ppermute | solution.py:56
  149.3 20.2 %copy-start = (f32[2048,4096]{1,0:T(8,128)S(1)}, f32[2048,4096]{1,0:T(8,128)}, u32[]{:S(2)}) copy-start(f32[2048,4096]{1,0:T(8,128)} %get-tuple-element.59) | copy-start | bytes 100663296
  177.1 10.5 %collective-permute-start.17 = (f32[2,4096]{1,0:T(2,128)S(1)}, f32[2,4096]{1,0:T(2,128)S(1)}, u32[]{:S(2)}, u32[]{:S(2)}) collective-permute-start(f32[2,4096]{1,0:T(2,128)S(1)} %pad_maximum_fusion.3), channel_id=1, source_target_pairs={{0,8},{8,16},{16,24},{24,0},{32,40},{40,48},{48,56},{56,32},{64,72... | collective-permute-start | bytes 98312 | tf_op jit(solution)/shard_map/ppermute | solution.py:56
  180.5 7.9 %collective-permute-start.18 = (f32[2,4096]{1,0:T(2,128)S(1)}, f32[2,4096]{1,0:T(2,128)S(1)}, u32[]{:S(2)}, u32[]{:S(2)}) collective-permute-start(f32[2,4096]{1,0:T(2,128)S(1)} %pad_maximum_fusion.3), channel_id=1, source_target_pairs={{0,16},{8,24},{16,0},{24,8},{32,48},{40,56},{48,32},{56,40},{64,80... | collective-permute-start | bytes 98312 | tf_op jit(solution)/shard_map/ppermute | solution.py:56
  186.2 3.9 %collective-permute-start.19 = (f32[2,4096]{1,0:T(2,128)S(1)}, f32[2,4096]{1,0:T(2,128)S(1)}, u32[]{:S(2)}, u32[]{:S(2)}) collective-permute-start(f32[2,4096]{1,0:T(2,128)S(1)} %pad_maximum_fusion.3), channel_id=1, source_target_pairs={{0,24},{8,0},{16,8},{24,16},{32,56},{40,32},{48,40},{56,48},{64,88... | collective-permute-start | bytes 98312 | tf_op jit(solution)/shard_map/ppermute | solution.py:56
  190.3 5.4 %collective-permute-start.20 = (f32[2,4096]{1,0:T(2,128)S(1)}, f32[2,4096]{1,0:T(2,128)S(1)}, u32[]{:S(2)}, u32[]{:S(2)}) collective-permute-start(f32[2,4096]{1,0:T(2,128)S(1)} %pad_maximum_fusion.4), channel_id=1, source_target_pairs={{0,32},{8,40},{16,48},{24,56},{32,64},{40,72},{48,80},{56,88},{64,... | collective-permute-start | bytes 98312 | tf_op jit(solution)/shard_map/ppermute | solution.py:56
  190.4 5.4 %collective-permute-start.21 = (f32[2,4096]{1,0:T(2,128)S(1)}, f32[2,4096]{1,0:T(2,128)S(1)}, u32[]{:S(2)}, u32[]{:S(2)}) collective-permute-start(f32[2,4096]{1,0:T(2,128)S(1)} %pad_maximum_fusion.4), channel_id=1, source_target_pairs={{0,64},{8,72},{16,80},{24,88},{32,96},{40,104},{48,112},{56,120},{... | collective-permute-start | bytes 98312 | tf_op jit(solution)/shard_map/ppermute | solution.py:56
  193.2 4.1 %collective-permute-start.22 = (f32[2,4096]{1,0:T(2,128)S(1)}, f32[2,4096]{1,0:T(2,128)S(1)}, u32[]{:S(2)}, u32[]{:S(2)}) collective-permute-start(f32[2,4096]{1,0:T(2,128)S(1)} %pad_maximum_fusion.4), channel_id=1, source_target_pairs={{0,96},{8,104},{16,112},{24,120},{32,0},{40,8},{48,16},{56,24},{64... | collective-permute-start | bytes 98312 | tf_op jit(solution)/shard_map/ppermute | solution.py:56
  208.7 1.3 collective-permute-start.23
  210.1 5.0 %collective-permute-start.24 = (f32[2,2048]{1,0:T(2,128)S(1)}, f32[2,2048]{1,0:T(2,128)S(1)}, u32[]{:S(2)}, u32[]{:S(2)}) collective-permute-start(f32[2,2048]{1,0:T(2,128)S(1)} %pad_maximum_fusion.12), channel_id=1, source_target_pairs={{0,2},{1,3},{2,4},{3,5},{4,6},{5,7},{6,0},{7,1},{8,10},{9,11},{10,... | collective-permute-start | bytes 49160 | tf_op jit(solution)/shard_map/ppermute | solution.py:56
  210.4 5.7 %collective-permute-start.25 = (f32[2,2048]{1,0:T(2,128)S(1)}, f32[2,2048]{1,0:T(2,128)S(1)}, u32[]{:S(2)}, u32[]{:S(2)}) collective-permute-start(f32[2,2048]{1,0:T(2,128)S(1)} %pad_maximum_fusion.12), channel_id=1, source_target_pairs={{0,4},{1,5},{2,6},{3,7},{4,0},{5,1},{6,2},{7,3},{8,12},{9,13},{10,... | collective-permute-start | bytes 49160 | tf_op jit(solution)/shard_map/ppermute | solution.py:56
  214.2 3.7 %collective-permute-start.26 = (f32[2,2048]{1,0:T(2,128)S(1)}, f32[2,2048]{1,0:T(2,128)S(1)}, u32[]{:S(2)}, u32[]{:S(2)}) collective-permute-start(f32[2,2048]{1,0:T(2,128)S(1)} %pad_maximum_fusion.12), channel_id=1, source_target_pairs={{0,6},{1,7},{2,0},{3,1},{4,2},{5,3},{6,4},{7,5},{8,14},{9,15},{10,... | collective-permute-start | bytes 49160 | tf_op jit(solution)/shard_map/ppermute | solution.py:56
  230.4 5.5 %collective-permute-start.27 = (f32[2,4096]{1,0:T(2,128)S(1)}, f32[2,4096]{1,0:T(2,128)S(1)}, u32[]{:S(2)}, u32[]{:S(2)}) collective-permute-start(f32[2,4096]{1,0:T(2,128)S(1)} %pad_maximum_fusion.5), channel_id=1, source_target_pairs={{0,8},{8,16},{16,24},{24,0},{32,40},{40,48},{48,56},{56,32},{64,72... | collective-permute-start | bytes 98312 | tf_op jit(solution)/shard_map/ppermute | solution.py:56
  231.6 6.1 %collective-permute-start.28 = (f32[2,4096]{1,0:T(2,128)S(1)}, f32[2,4096]{1,0:T(2,128)S(1)}, u32[]{:S(2)}, u32[]{:S(2)}) collective-permute-start(f32[2,4096]{1,0:T(2,128)S(1)} %pad_maximum_fusion.5), channel_id=1, source_target_pairs={{0,16},{8,24},{16,0},{24,8},{32,48},{40,56},{48,32},{56,40},{64,80... | collective-permute-start | bytes 98312 | tf_op jit(solution)/shard_map/ppermute | solution.py:56
  235.5 3.9 %collective-permute-start.29 = (f32[2,4096]{1,0:T(2,128)S(1)}, f32[2,4096]{1,0:T(2,128)S(1)}, u32[]{:S(2)}, u32[]{:S(2)}) collective-permute-start(f32[2,4096]{1,0:T(2,128)S(1)} %pad_maximum_fusion.5), channel_id=1, source_target_pairs={{0,24},{8,0},{16,8},{24,16},{32,56},{40,32},{48,40},{56,48},{64,88... | collective-permute-start | bytes 98312 | tf_op jit(solution)/shard_map/ppermute | solution.py:56
  239.5 5.5 %collective-permute-start.30 = (f32[2,4096]{1,0:T(2,128)S(1)}, f32[2,4096]{1,0:T(2,128)S(1)}, u32[]{:S(2)}, u32[]{:S(2)}) collective-permute-start(f32[2,4096]{1,0:T(2,128)S(1)} %pad_maximum_fusion.6), channel_id=1, source_target_pairs={{0,32},{8,40},{16,48},{24,56},{32,64},{40,72},{48,80},{56,88},{64,... | collective-permute-start | bytes 98312 | tf_op jit(solution)/shard_map/ppermute | solution.py:56
  240.8 6.1 %collective-permute-start.31 = (f32[2,4096]{1,0:T(2,128)S(1)}, f32[2,4096]{1,0:T(2,128)S(1)}, u32[]{:S(2)}, u32[]{:S(2)}) collective-permute-start(f32[2,4096]{1,0:T(2,128)S(1)} %pad_maximum_fusion.6), channel_id=1, source_target_pairs={{0,64},{8,72},{16,80},{24,88},{32,96},{40,104},{48,112},{56,120},{... | collective-permute-start | bytes 98312 | tf_op jit(solution)/shard_map/ppermute | solution.py:56
  244.6 3.9 %collective-permute-start.32 = (f32[2,4096]{1,0:T(2,128)S(1)}, f32[2,4096]{1,0:T(2,128)S(1)}, u32[]{:S(2)}, u32[]{:S(2)}) collective-permute-start(f32[2,4096]{1,0:T(2,128)S(1)} %pad_maximum_fusion.6), channel_id=1, source_target_pairs={{0,96},{8,104},{16,112},{24,120},{32,0},{40,8},{48,16},{56,24},{64... | collective-permute-start | bytes 98312 | tf_op jit(solution)/shard_map/ppermute | solution.py:56
  259.9 1.3 collective-permute-start.33
  261.3 5.0 %collective-permute-start.34 = (f32[2,2048]{1,0:T(2,128)S(1)}, f32[2,2048]{1,0:T(2,128)S(1)}, u32[]{:S(2)}, u32[]{:S(2)}) collective-permute-start(f32[2,2048]{1,0:T(2,128)S(1)} %pad_maximum_fusion.14), channel_id=1, source_target_pairs={{0,2},{1,3},{2,4},{3,5},{4,6},{5,7},{6,0},{7,1},{8,10},{9,11},{10,... | collective-permute-start | bytes 49160 | tf_op jit(solution)/shard_map/ppermute | solution.py:56
  261.4 5.3 %collective-permute-start.35 = (f32[2,2048]{1,0:T(2,128)S(1)}, f32[2,2048]{1,0:T(2,128)S(1)}, u32[]{:S(2)}, u32[]{:S(2)}) collective-permute-start(f32[2,2048]{1,0:T(2,128)S(1)} %pad_maximum_fusion.14), channel_id=1, source_target_pairs={{0,4},{1,5},{2,6},{3,7},{4,0},{5,1},{6,2},{7,3},{8,12},{9,13},{10,... | collective-permute-start | bytes 49160 | tf_op jit(solution)/shard_map/ppermute | solution.py:56
  264.2 3.7 %collective-permute-start.36 = (f32[2,2048]{1,0:T(2,128)S(1)}, f32[2,2048]{1,0:T(2,128)S(1)}, u32[]{:S(2)}, u32[]{:S(2)}) collective-permute-start(f32[2,2048]{1,0:T(2,128)S(1)} %pad_maximum_fusion.14), channel_id=1, source_target_pairs={{0,6},{1,7},{2,0},{3,1},{4,2},{5,3},{6,4},{7,5},{8,14},{9,15},{10,... | collective-permute-start | bytes 49160 | tf_op jit(solution)/shard_map/ppermute | solution.py:56
  268.0 4.8 %copy-start.4 = (f32[2048]{0:T(1024)}, f32[2048]{0:T(1024)S(1)}, u32[]{:S(2)}) copy-start(f32[2048]{0:T(1024)S(1)} %multiply_subtract_fusion.4) | copy-start | bytes 24580
  280.5 5.2 %collective-permute-start.37 = (f32[2,4096]{1,0:T(2,128)S(1)}, f32[2,4096]{1,0:T(2,128)S(1)}, u32[]{:S(2)}, u32[]{:S(2)}) collective-permute-start(f32[2,4096]{1,0:T(2,128)S(1)} %pad_maximum_fusion.7), channel_id=1, source_target_pairs={{0,8},{8,16},{16,24},{24,0},{32,40},{40,48},{48,56},{56,32},{64,72... | collective-permute-start | bytes 98312 | tf_op jit(solution)/shard_map/ppermute | solution.py:56
  280.6 5.5 %collective-permute-start.38 = (f32[2,4096]{1,0:T(2,128)S(1)}, f32[2,4096]{1,0:T(2,128)S(1)}, u32[]{:S(2)}, u32[]{:S(2)}) collective-permute-start(f32[2,4096]{1,0:T(2,128)S(1)} %pad_maximum_fusion.7), channel_id=1, source_target_pairs={{0,16},{8,24},{16,0},{24,8},{32,48},{40,56},{48,32},{56,40},{64,80... | collective-permute-start | bytes 98312 | tf_op jit(solution)/shard_map/ppermute | solution.py:56
  283.2 3.9 %collective-permute-start.39 = (f32[2,4096]{1,0:T(2,128)S(1)}, f32[2,4096]{1,0:T(2,128)S(1)}, u32[]{:S(2)}, u32[]{:S(2)}) collective-permute-start(f32[2,4096]{1,0:T(2,128)S(1)} %pad_maximum_fusion.7), channel_id=1, source_target_pairs={{0,24},{8,0},{16,8},{24,16},{32,56},{40,32},{48,40},{56,48},{64,88... | collective-permute-start | bytes 98312 | tf_op jit(solution)/shard_map/ppermute | solution.py:56
  287.3 5.2 %collective-permute-start.40 = (f32[2,4096]{1,0:T(2,128)S(1)}, f32[2,4096]{1,0:T(2,128)S(1)}, u32[]{:S(2)}, u32[]{:S(2)}) collective-permute-start(f32[2,4096]{1,0:T(2,128)S(1)} %pad_maximum_fusion.8), channel_id=1, source_target_pairs={{0,32},{8,40},{16,48},{24,56},{32,64},{40,72},{48,80},{56,88},{64,... | collective-permute-start | bytes 98312 | tf_op jit(solution)/shard_map/ppermute | solution.py:56
  287.4 5.5 %collective-permute-start.41 = (f32[2,4096]{1,0:T(2,128)S(1)}, f32[2,4096]{1,0:T(2,128)S(1)}, u32[]{:S(2)}, u32[]{:S(2)}) collective-permute-start(f32[2,4096]{1,0:T(2,128)S(1)} %pad_maximum_fusion.8), channel_id=1, source_target_pairs={{0,64},{8,72},{16,80},{24,88},{32,96},{40,104},{48,112},{56,120},{... | collective-permute-start | bytes 98312 | tf_op jit(solution)/shard_map/ppermute | solution.py:56
  290.1 3.9 %collective-permute-start.42 = (f32[2,4096]{1,0:T(2,128)S(1)}, f32[2,4096]{1,0:T(2,128)S(1)}, u32[]{:S(2)}, u32[]{:S(2)}) collective-permute-start(f32[2,4096]{1,0:T(2,128)S(1)} %pad_maximum_fusion.8), channel_id=1, source_target_pairs={{0,96},{8,104},{16,112},{24,120},{32,0},{40,8},{48,16},{56,24},{64... | collective-permute-start | bytes 98312 | tf_op jit(solution)/shard_map/ppermute | solution.py:56
